TPU v7x, 32 devices: a whole 2x2x4 slice. The times are simulated.
32 devices in a mesh: groups: 2 (over y), patch: 4 (over z), chan: 2 (over x), col: 2 (over core).
Axes of the slice: x: 2, y: 2, z: 4, core: 2. Of those that a mesh axis runs over, the one named last changes fastest.
Arguments:
- features: bfloat16 [1280, 48, 256], P('chan', ('groups', 'patch'), 'col'), parts along dimension 1, may hold values from -16 to 16
- cache_codes: bfloat16 [1280, 16, 256], P('chan', ('groups', 'patch'), 'col'), parts along dimension 1, may hold values from -127 to 127
- cache_scale: float32 [16, 256], P(('groups', 'patch'), 'col'), parts along dimension 0, may hold values from 0.001 to 0.01
- step_index: int32 [2], P('groups'), parts along dimension 0, may hold values from 0 to 999
- gn1_gain: float32 [1280], P('chan'), may hold values from 0.1 to 1.9
- gn1_shift: float32 [1280], P('chan'), may hold values from -3 to 3
- conv1_weight: bfloat16 [3, 3, 1280, 1280], P(None, None, 'patch', 'chan'), may hold values from -0.0546875 to 0.0546875
- conv1_bias: float32 [1280], P('chan'), may hold values from -3 to 3
- temb_weight: bfloat16 [1280, 1280], P(None, 'chan'), may hold values from -0.15625 to 0.15625
- gn2_gain: float32 [1280], P('chan'), may hold values from 0.1 to 1.9
- gn2_shift: float32 [1280], P('chan'), may hold values from -3 to 3
- conv2_weight: bfloat16 [3, 3, 1280, 1280], P(None, None, 'patch', 'chan'), may hold values from -0.0546875 to 0.0546875
- conv2_bias: float32 [1280], P('chan'), may hold values from -3 to 3
Outputs:
- block_out: bfloat16 [1280, 48, 256], P('chan', ('groups', 'patch'), 'col'), parts along dimension 1
There are 2 independent parts, one for each index of `groups`. A program takes and returns all parts, laid end to end along the dimension named above; an argument that names none is the same for every part. Nothing has to cross between parts.
All inputs are finite; a program needn't handle non-finite values.
Results may differ from a plain program's by a relative error of at most 0.009.
Values may be sent and summed in bfloat16 or wider, within the bound.
No kernel may reach another device: no remote copies, remote signals or barrier semaphores. Data moves between devices by JAX's collectives and lax.ppermute only.
A program may use at most 128 MiB of HBM per device.

v0:
```python
import math

import jax
import jax.numpy as jnp
from jax import lax
from jax.sharding import PartitionSpec as P

GROUPS = 32


norm_epsilon = 1e-05


def extended(value, sides, width):
    for axis, dim in sides:
        count, length = (lax.axis_size(axis), value.shape[dim])
        up = [(i, (i + 1) % count) for i in range(count - 1)]
        down = [(j, i) for i, j in up]
        last = lax.slice_in_dim(value, length - width, length, axis=dim)
        leading = lax.slice_in_dim(value, 0, width, axis=dim)
        before = lax.ppermute(last, axis, up)
        after = lax.ppermute(leading, axis, down)
        value = jnp.concatenate([before, value, after], axis=dim)
    return value


def group_moments(values, group_count, cell_total):
    grouped = values.reshape(group_count, -1)
    local_sums = (jnp.sum(grouped, axis=1), jnp.sum(grouped * grouped, axis=1))
    totals = lax.psum((local_sums[0], local_sums[1]), ("patch", "col"))
    group_mean = totals[0] / cell_total
    group_var = totals[1] / cell_total - group_mean * group_mean
    return (group_mean, lax.rsqrt(group_var + norm_epsilon))


def activate(values, group_mean, inv_std, gain_vec, shift_vec):
    channels = values.shape[0]
    width = channels // group_mean.shape[0]
    shape_tail = (channels,) + (1,) * (values.ndim - 1)
    mean_chan = jnp.repeat(group_mean, width).reshape(shape_tail)
    inv_chan = jnp.repeat(inv_std, width).reshape(shape_tail)
    normed = (values - mean_chan) * inv_chan * gain_vec.reshape(shape_tail) + shift_vec.reshape(
        shape_tail
    )
    return jax.nn.silu(normed)


def conv_sum(padded, weights):
    in_chans, height_pad, width_pad = padded.shape
    height = height_pad - 2
    width = width_pad - 2
    out_block = weights.shape[2]
    out_chans = out_block * lax.axis_size("patch") // lax.axis_size("chan")
    gathered = lax.all_gather(weights, "patch", axis=2, tiled=True)
    slabs = [padded[:, :, col_off : col_off + width] for col_off in range(3)]
    total = jnp.zeros((out_chans * lax.axis_size("chan"), height, width), jnp.float32)
    for row_off in range(3):
        for col_off in range(3):
            window = slabs[col_off][:, row_off : row_off + height, :]
            total = total + jnp.einsum(
                "oc,chw->ohw",
                gathered[row_off, col_off],
                window,
                preferred_element_type=jnp.float32,
            )
    return lax.psum_scatter(
        total.astype(jnp.bfloat16), "chan", scatter_dimension=0, tiled=True
    ).astype(jnp.float32)


def time_bias(step_index, temb_weight):
    half_width = temb_weight.shape[0] // 2
    freqs = jnp.exp(-math.log(10000.0) * jnp.arange(half_width).astype(jnp.float32) / half_width)
    angles = step_index[0].astype(jnp.float32) * freqs
    embed = jnp.concatenate([jnp.cos(angles), jnp.sin(angles)])
    gated = jax.nn.silu(embed).astype(jnp.bfloat16)
    return jnp.dot(gated[None, :], temb_weight, preferred_element_type=jnp.float32)[0]


def on_device(
    features,
    cache_codes,
    cache_scale,
    step_index,
    gn1_gain,
    gn1_shift,
    conv1_weight,
    conv1_bias,
    temb_weight,
    gn2_gain,
    gn2_shift,
    conv2_weight,
    conv2_bias,
):
    channels, rows_here, cols_here = features.shape
    patches = lax.axis_size("patch")
    group_count = GROUPS // lax.axis_size("chan")
    cell_total = channels // group_count * rows_here * patches * cols_here * lax.axis_size("col")
    feat32 = features.astype(jnp.float32)
    mean_one, inv_one = group_moments(feat32, group_count, cell_total)
    own_act = activate(feat32, mean_one, inv_one, gn1_gain, gn1_shift)
    stale = cache_codes.astype(jnp.float32) * cache_scale[None, :, :]
    rim_act = activate(stale, mean_one, inv_one, gn1_gain, gn1_shift)
    where_patch = lax.axis_index("patch")
    upper_rim = rim_act[:, 0:1, :] * (where_patch > 0).astype(jnp.float32)
    lower_rim = rim_act[:, 1:2, :] * (where_patch < patches - 1).astype(jnp.float32)
    block_one = jnp.concatenate([upper_rim, own_act, lower_rim], axis=1).astype(jnp.bfloat16)
    padded_one = extended(block_one, (("col", 2),), 1)
    sum_one = conv_sum(padded_one, conv1_weight)
    temb_bias = time_bias(step_index, temb_weight)
    hidden = (sum_one + conv1_bias[:, None, None] + temb_bias[:, None, None]).astype(jnp.bfloat16)
    hidden32 = hidden.astype(jnp.float32)
    mean_two, inv_two = group_moments(hidden32, group_count, cell_total)
    act_two = activate(hidden32, mean_two, inv_two, gn2_gain, gn2_shift).astype(jnp.bfloat16)
    padded_two = extended(act_two, (("patch", 1), ("col", 2)), 1)
    sum_two = conv_sum(padded_two, conv2_weight)
    return (sum_two + conv2_bias[:, None, None] + feat32).astype(jnp.bfloat16)


def solution(mesh):
    return jax.shard_map(
        on_device,
        mesh=mesh,
        in_specs=(
            P("chan", ("groups", "patch"), "col"),
            P("chan", ("groups", "patch"), "col"),
            P(("groups", "patch"), "col"),
            P("groups"),
            P("chan"),
            P("chan"),
            P(None, None, "patch", "chan"),
            P("chan"),
            P(None, "chan"),
            P("chan"),
            P("chan"),
            P(None, None, "patch", "chan"),
            P("chan"),
        ),
        out_specs=P("chan", ("groups", "patch"), "col"),
        check_vma=False,
    )
```

profile of v0, /device:TPU:0, one launch (start us, length us, event | category | flops | bytes accessed | tf_op | source)
XLA Modules:
  0.0 675.0 jit_solution(11318264559550244691)
XLA Ops:
  9.7 18.2 %all-reduce.1 = (f32[16]{0:T(128)S(1)}, f32[16]{0:T(128)S(1)}) all-reduce(f32[16]{0:T(128)S(1)} %reduce_sum.54, f32[16]{0:T(128)S(1)} %reduce_sum.51), channel_id=1, replica_groups=mesh['groups'=2,'patch'=4,'chan'=2,'col'=2] {'patch','col'}, use_global_device_ids=true, to_apply=%region_5.6 | all-reduce | flops 32 | bytes 256 | tf_op jit(solution)/shard_map/psum | solution.py:30
  36.8 228.5 %all-gather.3.cloned.1.call-done = bf16[3,3,1280,640]{3,2,1,0:T(8,128)(2,1)} async-done(((bf16[3,3,320,640]{3,2,1,0:T(8,128)(2,1)}), bf16[3,3,1280,640]{3,2,1,0:T(8,128)(2,1)}) %all-gather.3.cloned.1.call-update) | async-done | bytes 14745616 | tf_op jit(solution)/shard_map/all_gather | solution.py:54
  265.2 3.5 fusion.34
  268.8 3.3 fusion.31
  272.0 3.2 fusion.32
  275.2 3.2 fusion.30
  278.4 5.0 fusion.29
  283.4 3.3 convolution_add_fusion.4
  286.7 3.2 fusion.33
  289.9 3.4 convolution_add_fusion.3
  293.3 5.9 fusion
  299.2 4.0 copy.27
  305.1 26.9 %reduce-scatter.7.cloned.1.call-done = bf16[640,768]{1,0:T(8,128)(2,1)} async-done(((bf16[1280,768]{1,0:T(8,128)(2,1)}), bf16[640,768]{1,0:T(8,128)(2,1)}) %reduce-scatter.7.cloned.1.call-update) | async-done | bytes 983056
  334.4 16.6 %all-reduce = (f32[16]{0:T(128)S(1)}, f32[16]{0:T(128)S(1)}) all-reduce(f32[16]{0:T(128)S(1)} %reduce_sum.75, f32[16]{0:T(128)S(1)} %reduce_sum.72), channel_id=1, replica_groups=mesh['groups'=2,'patch'=4,'chan'=2,'col'=2] {'patch','col'}, use_global_device_ids=true, to_apply=%region_12.13 | all-reduce | flops 32 | bytes 256 | tf_op jit(solution)/shard_map/psum | solution.py:30
  356.2 234.5 %all-gather.5.cloned.1.call-done = bf16[3,3,1280,640]{3,2,1,0:T(8,128)(2,1)} async-done(((bf16[3,3,320,640]{3,2,1,0:T(8,128)(2,1)}), bf16[3,3,1280,640]{3,2,1,0:T(8,128)(2,1)}) %all-gather.5.cloned.1.call-update) | async-done | bytes 14745616 | tf_op jit(solution)/shard_map/all_gather | solution.py:54
  600.3 3.2 fusion.23
  604.0 3.2 fusion.26
  607.2 5.0 fusion.24
  612.2 3.2 convolution_add_fusion.1
  615.4 3.2 fusion.27
  618.6 3.4 convolution_add_fusion
  622.0 5.9 add_convert_fusion
  627.9 4.0 copy.29
  631.9 29.5 %reduce-scatter.9.cloned.1.call-done = bf16[640,768]{1,0:T(8,128)(2,1)} async-done(((bf16[1280,768]{1,0:T(8,128)(2,1)}), bf16[640,768]{1,0:T(8,128)(2,1)}) %reduce-scatter.9.cloned.1.call-update) | async-done | bytes 983056
  (91 shorter events, 37.6 us)
Async XLA Ops:
  6.5 298.2 %copy-start = (bf16[1280,640]{1,0:T(8,128)(2,1)S(1)}, bf16[1280,640]{1,0:T(8,128)(2,1)}, u32[]{:S(2)}) copy-start(bf16[1280,640]{1,0:T(8,128)(2,1)} %param.21) | copy-start | bytes 4915204
  6.5 258.7 %all-gather.3.cloned.1.call-start = ((), (), s32[]{:S(2)}) async-start(), calls=%async_computation.2 | async-start | bytes 18432000 | tf_op jit(solution)/shard_map/all_gather | solution.py:54
  7.3 21.0 %copy-start.7 = (bf16[640,2,128]{2,1,0:T(2,128)(2,1)S(1)}, bf16[640,2,128]{2,1,0:T(2,128)(2,1)}, u32[]{:S(2)}) copy-start(bf16[640,2,128]{2,1,0:T(2,128)(2,1)} %param.14) | copy-start | bytes 983044
  7.3 21.9 %copy-start.8 = (f32[640]{0:T(1024)S(1)}, f32[640]{0:T(1024)}, u32[]{:S(2)}) copy-start(f32[640]{0:T(1024)} %param.18) | copy-start | bytes 7684
  7.3 21.9 %copy-start.9 = (f32[640]{0:T(1024)S(1)}, f32[640]{0:T(1024)}, u32[]{:S(2)}) copy-start(f32[640]{0:T(1024)} %param.17) | copy-start | bytes 7684
  7.3 21.9 %copy-start.14 = (f32[2,128]{1,0:T(2,128)S(1)}, f32[2,128]{1,0:T(2,128)}, u32[]{:S(2)}) copy-start(f32[2,128]{1,0:T(2,128)} %param.15) | copy-start | bytes 3076
  7.3 324.7 %reduce-scatter.7.cloned.1.call-start = ((), (), s32[]{:S(2)}) async-start(), calls=%async_computation.4 | async-start | bytes 2949120
  30.3 4.4 copy-start.3
  30.3 2.8 collective-permute-start
  31.6 3.1 collective-permute-start.1
  265.2 3.5 copy-start.4
  283.4 3.3 copy-start.5
  303.2 287.5 %all-gather.5.cloned.1.call-start = ((), (), s32[]{:S(2)}) async-start(), calls=%async_computation.3 | async-start | bytes 18432000 | tf_op jit(solution)/shard_map/all_gather | solution.py:54
  303.9 29.6 %copy-start.10 = (f32[640]{0:T(1024)S(1)}, f32[640]{0:T(1024)}, u32[]{:S(2)}) copy-start(f32[640]{0:T(1024)} %param.20) | copy-start | bytes 7684
  304.0 357.5 %reduce-scatter.9.cloned.1.call-start = ((), (), s32[]{:S(2)}) async-start(), calls=%async_computation.5 | async-start | bytes 2949120
  304.8 46.6 %copy-start.11 = (f32[640]{0:T(1024)S(1)}, f32[640]{0:T(1024)}, u32[]{:S(2)}) copy-start(f32[640]{0:T(1024)} %param.23) | copy-start | bytes 7684
  304.8 46.6 %copy-start.12 = (f32[640]{0:T(1024)S(1)}, f32[640]{0:T(1024)}, u32[]{:S(2)}) copy-start(f32[640]{0:T(1024)} %param.22) | copy-start | bytes 7684
  333.6 17.7 %copy-start.2 = (bf16[640,768]{0,1:T(8,128)(2,1)}, bf16[640,768]{0,1:T(8,128)(2,1)S(1)}, u32[]{:S(2)}) copy-start(bf16[640,768]{0,1:T(8,128)(2,1)S(1)} %copy.28) | copy-start | bytes 2949124
  353.6 240.3 %collective-permute-start.2 = (bf16[640,1,128]{0,2,1:T(8,128)(2,1)S(1)}, bf16[640,1,128]{0,2,1:T(8,128)(2,1)S(1)}, u32[]{:S(2)}, u32[]{:S(2)}) collective-permute-start(bf16[640,1,128]{0,2,1:T(8,128)(2,1)S(1)} %get-tuple-element.21), channel_id=1, source_target_pairs={{0,4},{4,8},{8,12},{1,5},{5,9},{9,13},{2,6},{6,10},{10,14},{3,7},{... | collective-permute-start | bytes 491528 | tf_op jit(solution)/shard_map/ppermute | solution.py:21
  354.9 239.0 %collective-permute-start.3 = (bf16[640,1,128]{0,2,1:T(8,128)(2,1)S(1)}, bf16[640,1,128]{0,2,1:T(8,128)(2,1)S(1)}, u32[]{:S(2)}, u32[]{:S(2)}) collective-permute-start(bf16[640,1,128]{0,2,1:T(8,128)(2,1)S(1)} %get-tuple-element.22), channel_id=1, source_target_pairs={{4,0},{8,4},{12,8},{5,1},{9,5},{13,9},{6,2},{10,6},{14,10},{7,3},{... | collective-permute-start | bytes 491528 | tf_op jit(solution)/shard_map/ppermute | solution.py:22
  593.9 9.5 %collective-permute-start.4 = (bf16[640,8,1]{0,2,1:T(2,128)(2,1)S(1)}, bf16[640,8,1]{0,2,1:T(2,128)(2,1)S(1)}, u32[]{:S(2)}, u32[]{:S(2)}) collective-permute-start(bf16[640,8,1]{0,2,1:T(2,128)(2,1)S(1)} %get-tuple-element.16), channel_id=1, source_target_pairs={{0,1},{2,3},{4,5},{6,7},{8,9},{10,11},{12,13},{14,15},{16,17},{18,... | collective-permute-start | bytes 30728 | tf_op jit(solution)/shard_map/ppermute | solution.py:21
  595.8 7.6 %collective-permute-start.5 = (bf16[640,8,1]{0,2,1:T(2,128)(2,1)S(1)}, bf16[640,8,1]{0,2,1:T(2,128)(2,1)S(1)}, u32[]{:S(2)}, u32[]{:S(2)}) collective-permute-start(bf16[640,8,1]{0,2,1:T(2,128)(2,1)S(1)} %get-tuple-element.15), channel_id=1, source_target_pairs={{1,0},{3,2},{5,4},{7,6},{9,8},{11,10},{13,12},{15,14},{17,16},{19,... | collective-permute-start | bytes 30728 | tf_op jit(solution)/shard_map/ppermute | solution.py:22
  631.9 31.8 %copy-start.13 = (f32[640]{0:T(1024)S(1)}, f32[640]{0:T(1024)}, u32[]{:S(2)}) copy-start(f32[640]{0:T(1024)} %param.25) | copy-start | bytes 7684
  663.7 4.8 copy-start.1
  (1 other events, 3.3 us)
Sparse Core Ops, SparseCore 0:
  8.9 256.2 all-gather.2
  303.3 28.6 reduce-scatter.6
  333.6 257.0 all-gather.4
  632.0 29.3 reduce-scatter.8
where the time goes:
time: 676 us; the launch traced here: 675 us
  waiting for transfers between devices  522 us (77%)
  matrix products  67.6 us (10%)
  blocking collectives  34.8 us (5%)
  local copies, waits for them, and re-layouts  17.5 us (3%)
  between operations  14.3 us (2%)
  other arithmetic  9.64 us (1%)
  starting transfers between devices  8.68 us (1%)
    all_gather x2, waiting for transfers between devices, conv_sum(): gathered = lax.all_gather(weights, 'patch', axis=2, tiled=True)  463 us
    dot_general x18, matrix products, conv_sum(): jnp.einsum('oc,chw->ohw', gathered[row_off, col_off], window, preferred_e...  67.2 us
    unnamed x6, waiting for transfers between devices  57.9 us
    psum x2, blocking collectives, group_moments(): totals = lax.psum((local_sums[0], local_sums[1]), ('patch', 'col'))  34.8 us
    unnamed x36, local copies, waits for them, and re-layouts  14.3 us
  transfers between devices with their start and end apart: 10, of which 5 were waited for; matrix products, arithmetic and copies ran while one was open for 3% of the time, Pallas kernels for 0%

commit v1 on v0

--- a/solution.py
+++ b/solution.py
@@ -45,27 +45,77 @@
     return jax.nn.silu(normed)
 
 
-def conv_sum(padded, weights):
+def swap(value, axis):
+    return lax.ppermute(value, axis, [(0, 1), (1, 0)])
+
+
+def fetch_weights(weights):
+    taps = weights.shape[0] * weights.shape[1]
+    out_block, in_block = weights.shape[2], weights.shape[3]
+    flat = weights.reshape(taps, out_block, in_block)
+    share_y = lax.axis_size("groups") == 2
+    n_y = 2 if share_y else 1
+    n_c = lax.axis_size("col")
+    y_id = lax.axis_index("groups") if share_y else 0
+    c_id = lax.axis_index("col")
+    piece = out_block // (n_y * n_c)
+    own = y_id * n_c + c_id
+    mine = lax.dynamic_slice_in_dim(flat, own * piece, piece, axis=1)
+    got = lax.all_gather(mine, "patch", axis=0, tiled=False)
+    slots, ids = [got], [own]
+    if share_y:
+        slots.append(swap(got, "groups"))
+        ids.append((1 - y_id) * n_c + c_id)
+    if n_c == 2:
+        for i in range(len(slots)):
+            slots.append(swap(slots[i], "col"))
+            ids.append(ids[i] - c_id + (1 - c_id))
+    return slots, ids
+
+
+def conv_slots(padded, slots):
     in_chans, height_pad, width_pad = padded.shape
     height = height_pad - 2
     width = width_pad - 2
-    out_block = weights.shape[2]
-    out_chans = out_block * lax.axis_size("patch") // lax.axis_size("chan")
-    gathered = lax.all_gather(weights, "patch", axis=2, tiled=True)
-    slabs = [padded[:, :, col_off : col_off + width] for col_off in range(3)]
-    total = jnp.zeros((out_chans * lax.axis_size("chan"), height, width), jnp.float32)
-    for row_off in range(3):
-        for col_off in range(3):
-            window = slabs[col_off][:, row_off : row_off + height, :]
-            total = total + jnp.einsum(
-                "oc,chw->ohw",
-                gathered[row_off, col_off],
-                window,
-                preferred_element_type=jnp.float32,
-            )
-    return lax.psum_scatter(
-        total.astype(jnp.bfloat16), "chan", scatter_dimension=0, tiled=True
-    ).astype(jnp.float32)
+    windows = [
+        [padded[:, a : a + height, b : b + width] for b in range(3)] for a in range(3)
+    ]
+    outs = []
+    for got in slots:
+        total = None
+        for a in range(3):
+            for b in range(3):
+                term = jnp.einsum(
+                    "poc,chw->pohw",
+                    got[:, a * 3 + b],
+                    windows[a][b],
+                    preferred_element_type=jnp.float32,
+                )
+                total = term if total is None else total + term
+        outs.append(total.astype(jnp.bfloat16))
+    return jnp.stack(outs)
+
+
+def reduce_chan(parts, ids):
+    n_slots, blocks, piece, height, width = parts.shape
+    n_k = lax.axis_size("chan")
+    k = lax.axis_index("chan")
+    per = blocks // n_k
+    if n_k == 2:
+        mine = lax.dynamic_slice_in_dim(parts, k * per, per, axis=1)
+        other = lax.dynamic_slice_in_dim(parts, (1 - k) * per, per, axis=1)
+        total = mine.astype(jnp.float32) + swap(other, "chan").astype(jnp.float32)
+    else:
+        split = parts.reshape(n_slots, n_k, per, piece, height, width)
+        split = jnp.moveaxis(split, 1, 0)
+        got = lax.all_to_all(split, "chan", 0, 0, tiled=False)
+        total = jnp.sum(got.astype(jnp.float32), axis=0)
+    where = jnp.zeros((n_slots,), jnp.int32)
+    for slot, ident in enumerate(ids):
+        where = where.at[ident].set(slot)
+    ordered = jnp.take(total, where, axis=0)
+    ordered = jnp.moveaxis(ordered, 0, 1)
+    return ordered.reshape(per * n_slots * piece, height, width)
 
 
 def time_bias(step_index, temb_weight):
@@ -96,6 +146,8 @@
     patches = lax.axis_size("patch")
     group_count = GROUPS // lax.axis_size("chan")
     cell_total = channels // group_count * rows_here * patches * cols_here * lax.axis_size("col")
+    slots_one, ids_one = fetch_weights(conv1_weight)
+    slots_two, ids_two = fetch_weights(conv2_weight)
     feat32 = features.astype(jnp.float32)
     mean_one, inv_one = group_moments(feat32, group_count, cell_total)
     own_act = activate(feat32, mean_one, inv_one, gn1_gain, gn1_shift)
@@ -106,14 +158,14 @@
     lower_rim = rim_act[:, 1:2, :] * (where_patch < patches - 1).astype(jnp.float32)
     block_one = jnp.concatenate([upper_rim, own_act, lower_rim], axis=1).astype(jnp.bfloat16)
     padded_one = extended(block_one, (("col", 2),), 1)
-    sum_one = conv_sum(padded_one, conv1_weight)
+    sum_one = reduce_chan(conv_slots(padded_one, slots_one), ids_one)
     temb_bias = time_bias(step_index, temb_weight)
     hidden = (sum_one + conv1_bias[:, None, None] + temb_bias[:, None, None]).astype(jnp.bfloat16)
     hidden32 = hidden.astype(jnp.float32)
     mean_two, inv_two = group_moments(hidden32, group_count, cell_total)
     act_two = activate(hidden32, mean_two, inv_two, gn2_gain, gn2_shift).astype(jnp.bfloat16)
     padded_two = extended(act_two, (("patch", 1), ("col", 2)), 1)
-    sum_two = conv_sum(padded_two, conv2_weight)
+    sum_two = reduce_chan(conv_slots(padded_two, slots_two), ids_two)
     return (sum_two + conv2_bias[:, None, None] + feat32).astype(jnp.bfloat16)
 
 

time: 676 us -> 410 us (0.61)
  waiting for transfers between devices: 522 us -> 163 us
  matrix products: 67.6 us -> 105 us
  local copies, waits for them, and re-layouts: 17.5 us -> 42.7 us
  other arithmetic: 9.64 us -> 27.7 us
  starting transfers between devices: 8.68 us -> 15.5 us
    all_gather x2, waiting for transfers between devices: 463 us -> 97.5 us  [fetch_weights(): got = lax.all_gather(mine, 'patch', axis=0, tiled=False)]
    ppermute x0 -> x8, waiting for transfers between devices: none -> 64.9 us  [swap(): return lax.ppermute(value, axis, [(0, 1), (1, 0)])]
    unnamed x6 -> x2, waiting for transfers between devices: 57.9 us -> 0.03 us
    dot_general x18 -> x72, matrix products: 67.2 us -> 105 us  [conv_slots(): jnp.einsum('poc,chw->pohw', got[:, a * 3 + b], windows[a][b], preferred_e...]
    unnamed x36 -> x60, local copies, waits for them, and re-layouts: 14.3 us -> 3.55 us
    all_gather x0 -> x2, local copies, waits for them, and re-layouts: none -> 8.73 us  [fetch_weights(): got = lax.all_gather(mine, 'patch', axis=0, tiled=False)]
    ppermute x0 -> x8, starting transfers between devices: none -> 7.28 us  [swap(): return lax.ppermute(value, axis, [(0, 1), (1, 0)])]
    slice x1 -> x5, local copies, waits for them, and re-layouts: 0.03 us -> 7.3 us  [extended(): last = lax.slice_in_dim(value, length - width, length, axis=dim)]
  transfers between devices with their start and end apart: 10 -> 16, of which waited for: 5 -> 6; matrix products, arithmetic and copies ran while one was open for 3% -> 29% of each run, Pallas kernels for 0% -> 0%
where the time goes in v1:
time: 410 us; the launch traced here: 403 us
  waiting for transfers between devices  163 us (40%)
  matrix products  105 us (26%)
  local copies, waits for them, and re-layouts  42.7 us (10%)
  blocking collectives  33.5 us (8%)
  other arithmetic  27.7 us (7%)
  starting transfers between devices  15.5 us (4%)
  between operations  15.4 us (4%)
    dot_general x72, matrix products, conv_slots(): jnp.einsum('poc,chw->pohw', got[:, a * 3 + b], windows[a][b], preferred_e...  105 us
    all_gather x2, waiting for transfers between devices, fetch_weights(): got = lax.all_gather(mine, 'patch', axis=0, tiled=False)  97.5 us
    ppermute x8, waiting for transfers between devices, swap(): return lax.ppermute(value, axis, [(0, 1), (1, 0)])  64.9 us
    psum x2, blocking collectives, group_moments(): totals = lax.psum((local_sums[0], local_sums[1]), ('patch', 'col'))  33.5 us
    concatenate x3, other arithmetic, extended(): value = jnp.concatenate([before, value, after], axis=dim)  9.24 us
    all_gather x2, local copies, waits for them, and re-layouts, fetch_weights(): got = lax.all_gather(mine, 'patch', axis=0, tiled=False)  8.73 us
  transfers between devices with their start and end apart: 16, of which 6 were waited for; matrix products, arithmetic and copies ran while one was open for 29% of the time, Pallas kernels for 0%

profile of v1, /device:TPU:0, one launch (start us, length us, event | category | flops | bytes accessed | tf_op | source)
XLA Modules:
  0.0 402.6 jit_solution(16626125530148829790)
XLA Ops:
  12.0 18.8 %all-reduce.1 = (f32[16]{0:T(128)S(1)}, f32[16]{0:T(128)S(1)}) all-reduce(f32[16]{0:T(128)S(1)} %reduce_sum.54, f32[16]{0:T(128)S(1)} %reduce_sum.51), channel_id=1, replica_groups=mesh['groups'=2,'patch'=4,'chan'=2,'col'=2] {'patch','col'}, use_global_device_ids=true, to_apply=%region_5.6 | all-reduce | flops 32 | bytes 256 | tf_op jit(solution)/shard_map/psum | solution.py:30
  34.6 49.6 %all-gather.7.cloned.1.call-done = bf16[36,80,640]{2,1,0:T(8,128)(2,1)} async-done(((bf16[9,80,640]{2,1,0:T(8,128)(2,1)}), bf16[36,80,640]{2,1,0:T(8,128)(2,1)}) %all-gather.7.cloned.1.call-update) | async-done | bytes 3686416 | tf_op jit(solution)/shard_map/all_gather | solution.py:64
  84.2 4.3 %copy.134 = bf16[4,9,80,640]{3,2,0,1:T(8,128)(2,1)} copy(bf16[4,9,80,640]{3,2,1,0:T(8,128)(2,1)} %bitcast.595) | data formatting | bytes 7372800 | tf_op jit(solution)/shard_map/all_gather | solution.py:64
  102.5 5.3 %maximum_maximum_fusion = (bf16[640,8,129]{2,0,1:T(8,128)(2,1)}, bf16[640,8,129]{2,0,1:T(8,128)(2,1)}) fusion(bf16[640,1,128]{2,0,1:T(8,128)(2,1)S(1)} %get-tuple-element.107, bf16[640,6,128]{2,0,1:T(8,128)(2,1)S(1)} %fusion.19, bf16[640,1,128]{2,0,1:T(8,128)(2,1)S(1)} %copy-done.14, bf16[640,8,1]{2,0,1:T(8,128)(2,1)} %copy.137, bf16[640,8,1]{2,0,1:T(8,128)(2,1)} %copy.141), kind=kLoop, calls=%fused_computation.9 | loop fusion | flops 10567680 | bytes 3973120 | tf_op jit(solution)/shard_map/concatenate | solution.py:23
  108.9 47.9 %all-gather.5.cloned.1.call-done = bf16[36,80,640]{2,1,0:T(8,128)(2,1)} async-done(((bf16[9,80,640]{2,1,0:T(8,128)(2,1)}), bf16[36,80,640]{2,1,0:T(8,128)(2,1)}) %all-gather.5.cloned.1.call-update) | async-done | bytes 3686416 | tf_op jit(solution)/shard_map/all_gather | solution.py:64
  156.8 4.4 %copy.133 = bf16[4,9,80,640]{3,2,0,1:T(8,128)(2,1)} copy(bf16[4,9,80,640]{3,2,1,0:T(8,128)(2,1)} %bitcast.605) | data formatting | bytes 7372800 | tf_op jit(solution)/shard_map/all_gather | solution.py:64
  168.1 3.3 collective-permute-done.2
  210.3 38.9 %collective-permute-done.10 = bf16[4,9,80,640]{3,2,0,1:T(8,128)(2,1)} collective-permute-done((bf16[4,9,80,640]{3,2,0,1:T(8,128)(2,1)}, bf16[4,9,80,640]{3,2,0,1:T(8,128)(2,1)}, u32[]{:S(2)}, u32[]{:S(2)}) %collective-permute-start.10) | collective-permute-done | bytes 3686432 | tf_op jit(solution)/shard_map/ppermute | solution.py:49
  250.6 3.0 convert_add_fusion.2
  253.6 3.5 gather_fusion
  257.1 3.4 convert_reduce_fusion.1
  260.8 14.7 %all-reduce = (f32[16]{0:T(128)S(1)}, f32[16]{0:T(128)S(1)}) all-reduce(f32[16]{0:T(128)S(1)} %reduce_sum.75, f32[16]{0:T(128)S(1)} %reduce_sum.72), channel_id=1, replica_groups=mesh['groups'=2,'patch'=4,'chan'=2,'col'=2] {'patch','col'}, use_global_device_ids=true, to_apply=%region_11.13 | all-reduce | flops 32 | bytes 256 | tf_op jit(solution)/shard_map/psum | solution.py:30
  283.3 2.5 fusion.122
  285.8 2.5 fusion.115
  288.3 2.5 fusion.107
  299.9 2.5 fusion.125
  302.5 2.5 fusion.120
  305.0 2.6 fusion.118
  307.6 2.5 fusion.112
  312.7 2.5 fusion.104
  315.2 2.5 fusion.102
  322.5 3.7 maximum_maximum_fusion.1
  363.5 22.8 %collective-permute-done.13 = bf16[4,2,80,6,128]{4,2,3,1,0:T(8,128)(2,1)S(1)} collective-permute-done((bf16[4,2,80,6,128]{4,2,3,1,0:T(8,128)(2,1)S(1)}, bf16[4,2,80,6,128]{4,2,3,1,0:T(8,128)(2,1)S(1)}, u32[]{:S(2)}, u32[]{:S(2)}) %collective-permute-start.13) | collective-permute-done | bytes 983072 | tf_op jit(solution)/shard_map/ppermute | solution.py:49
  387.8 3.5 gather_fusion.1
  (231 shorter events, 137.3 us)
Async XLA Ops:
  6.5 242.6 %copy-start = (bf16[1280,640]{1,0:T(8,128)(2,1)S(1)}, bf16[1280,640]{1,0:T(8,128)(2,1)}, u32[]{:S(2)}) copy-start(bf16[1280,640]{1,0:T(8,128)(2,1)} %param.39) | copy-start | bytes 4915204
  6.5 77.7 %all-gather.7.cloned.1.call-start = ((), (), s32[]{:S(2)}) async-start(), calls=%async_computation.1 | async-start | bytes 4608000 | tf_op jit(solution)/shard_map/all_gather | solution.py:64
  8.9 22.2 %copy-start.23 = (f32[640]{0:T(1024)S(1)}, f32[640]{0:T(1024)}, u32[]{:S(2)}) copy-start(f32[640]{0:T(1024)} %param.36) | copy-start | bytes 7684
  8.9 22.2 %copy-start.24 = (f32[640]{0:T(1024)S(1)}, f32[640]{0:T(1024)}, u32[]{:S(2)}) copy-start(f32[640]{0:T(1024)} %param.35) | copy-start | bytes 7684
  8.9 22.2 %copy-start.29 = (f32[2,128]{1,0:T(2,128)S(1)}, f32[2,128]{1,0:T(2,128)}, u32[]{:S(2)}) copy-start(f32[2,128]{1,0:T(2,128)} %param.33) | copy-start | bytes 3076
  8.9 147.9 %all-gather.5.cloned.1.call-start = ((), (), s32[]{:S(2)}) async-start(), calls=%async_computation | async-start | bytes 4608000 | tf_op jit(solution)/shard_map/all_gather | solution.py:64
  88.6 82.9 %collective-permute-start.2 = (bf16[4,9,80,640]{3,2,0,1:T(8,128)(2,1)}, bf16[4,9,80,640]{3,2,0,1:T(8,128)(2,1)}, u32[]{:S(2)}, u32[]{:S(2)}) collective-permute-start(bf16[4,9,80,640]{3,2,0,1:T(8,128)(2,1)} %copy.134), channel_id=1, source_target_pairs={{0,16},{16,0},{1,17},{17,1},{2,18},{18,2},{3,19},{19,3},{4,20},{20... | collective-permute-start | bytes 11059208 | tf_op jit(solution)/shard_map/ppermute | solution.py:49
  92.9 9.6 %copy-start.14 = (bf16[640,1,128]{2,0,1:T(8,128)(2,1)S(1)}, bf16[640,1,128]{2,0,1:T(8,128)(2,1)}, u32[]{:S(2)}) copy-start(bf16[640,1,128]{2,0,1:T(8,128)(2,1)} %copy-done.13) | copy-start | bytes 491524
  94.9 4.4 %collective-permute-start = (bf16[640,8,1]{0,1,2:T(8,128)(2,1)S(1)}, bf16[640,8,1]{0,1,2:T(8,128)(2,1)S(1)}, u32[]{:S(2)}, u32[]{:S(2)}) collective-permute-start(bf16[640,8,1]{0,1,2:T(8,128)(2,1)S(1)} %copy.136), channel_id=1, source_target_pairs={{0,1},{2,3},{4,5},{6,7},{8,9},{10,11},{12,13},{14,15},{16,17},{18,... | collective-permute-start | bytes 30728 | tf_op jit(solution)/shard_map/ppermute | solution.py:21
  97.9 3.1 collective-permute-start.1
  107.9 73.1 %collective-permute-start.3 = (bf16[4,9,80,640]{3,2,0,1:T(8,128)(2,1)}, bf16[4,9,80,640]{3,2,0,1:T(8,128)(2,1)}, u32[]{:S(2)}, u32[]{:S(2)}) collective-permute-start(bf16[4,9,80,640]{3,2,0,1:T(8,128)(2,1)} %copy.134), channel_id=1, source_target_pairs={{0,1},{1,0},{2,3},{3,2},{4,5},{5,4},{6,7},{7,6},{8,9},{9,8},{10,11... | collective-permute-start | bytes 11059208 | tf_op jit(solution)/shard_map/ppermute | solution.py:49
  161.2 87.9 %collective-permute-start.10 = (bf16[4,9,80,640]{3,2,0,1:T(8,128)(2,1)}, bf16[4,9,80,640]{3,2,0,1:T(8,128)(2,1)}, u32[]{:S(2)}, u32[]{:S(2)}) collective-permute-start(bf16[4,9,80,640]{3,2,0,1:T(8,128)(2,1)} %copy.133), channel_id=1, source_target_pairs={{0,16},{16,0},{1,17},{17,1},{2,18},{18,2},{3,19},{19,3},{4,20},{20... | collective-permute-start | bytes 11059208 | tf_op jit(solution)/shard_map/ppermute | solution.py:49
  162.7 125.6 %collective-permute-start.11 = (bf16[4,9,80,640]{3,2,0,1:T(8,128)(2,1)}, bf16[4,9,80,640]{3,2,0,1:T(8,128)(2,1)}, u32[]{:S(2)}, u32[]{:S(2)}) collective-permute-start(bf16[4,9,80,640]{3,2,0,1:T(8,128)(2,1)} %copy.133), channel_id=1, source_target_pairs={{0,1},{1,0},{2,3},{3,2},{4,5},{5,4},{6,7},{7,6},{8,9},{9,8},{10,11... | collective-permute-start | bytes 11059208 | tf_op jit(solution)/shard_map/ppermute | solution.py:49
  171.4 29.5 %collective-permute-start.4 = (bf16[4,9,80,640]{3,2,0,1:T(8,128)(2,1)}, bf16[4,9,80,640]{3,2,0,1:T(8,128)(2,1)S(1)}, u32[]{:S(2)}, u32[]{:S(2)}) collective-permute-start(bf16[4,9,80,640]{3,2,0,1:T(8,128)(2,1)} %collective-permute-done.2), channel_id=1, source_target_pairs={{0,1},{1,0},{2,3},{3,2},{4,5},{5,4},{6,7},{7,6},{8,9},{9,8},{10,11... | collective-permute-start | bytes 11059208 | tf_op jit(solution)/shard_map/ppermute | solution.py:49
  208.0 41.7 %copy-start.25 = (f32[640]{0:T(1024)S(1)}, f32[640]{0:T(1024)}, u32[]{:S(2)}) copy-start(f32[640]{0:T(1024)} %param.38) | copy-start | bytes 7684
  208.0 41.8 %copy-start.27 = (f32[640]{0:T(1024)S(1)}, f32[640]{0:T(1024)}, u32[]{:S(2)}) copy-start(f32[640]{0:T(1024)} %param.40) | copy-start | bytes 7684
  208.0 41.9 %copy-start.26 = (f32[640]{0:T(1024)S(1)}, f32[640]{0:T(1024)}, u32[]{:S(2)}) copy-start(f32[640]{0:T(1024)} %param.41) | copy-start | bytes 7684
  208.0 42.5 %collective-permute-start.5 = (bf16[4,2,80,6,128]{4,2,3,1,0:T(8,128)(2,1)S(1)}, bf16[4,2,80,6,128]{4,2,3,1,0:T(8,128)(2,1)}, u32[]{:S(2)}, u32[]{:S(2)}) collective-permute-start(bf16[4,2,80,6,128]{4,2,3,1,0:T(8,128)(2,1)S(1)} %constant_dynamic-slice_fusion.1), channel_id=1, source_target_pairs={{0,2},{2,0},{1,3},{3,1},{4,6},{6,4},{5,7},{7,5},{8,10},{10,8},{9,1... | collective-permute-start | bytes 2949128 | tf_op jit(solution)/shard_map/ppermute | solution.py:49
  249.1 41.7 %collective-permute-start.12 = (bf16[4,9,80,640]{3,2,0,1:T(8,128)(2,1)}, bf16[4,9,80,640]{3,2,0,1:T(8,128)(2,1)}, u32[]{:S(2)}, u32[]{:S(2)}) collective-permute-start(bf16[4,9,80,640]{3,2,0,1:T(8,128)(2,1)} %collective-permute-done.10), channel_id=1, source_target_pairs={{0,1},{1,0},{2,3},{3,2},{4,5},{5,4},{6,7},{7,6},{8,9},{9,8},{10,11... | collective-permute-start | bytes 11059208 | tf_op jit(solution)/shard_map/ppermute | solution.py:49
  278.9 14.4 %collective-permute-start.6 = (bf16[640,1,128]{2,0,1:T(8,128)(2,1)S(1)}, bf16[640,1,128]{2,0,1:T(8,128)(2,1)S(1)}, u32[]{:S(2)}, u32[]{:S(2)}) collective-permute-start(bf16[640,1,128]{2,0,1:T(8,128)(2,1)S(1)} %get-tuple-element.104), channel_id=1, source_target_pairs={{0,4},{4,8},{8,12},{1,5},{5,9},{9,13},{2,6},{6,10},{10,14},{3,7},{... | collective-permute-start | bytes 491528 | tf_op jit(solution)/shard_map/ppermute | solution.py:21
  280.3 13.1 %collective-permute-start.7 = (bf16[640,1,128]{2,0,1:T(8,128)(2,1)S(1)}, bf16[640,1,128]{2,0,1:T(8,128)(2,1)S(1)}, u32[]{:S(2)}, u32[]{:S(2)}) collective-permute-start(bf16[640,1,128]{2,0,1:T(8,128)(2,1)S(1)} %get-tuple-element.105), channel_id=1, source_target_pairs={{4,0},{8,4},{12,8},{5,1},{9,5},{13,9},{6,2},{10,6},{14,10},{7,3},{... | collective-permute-start | bytes 491528 | tf_op jit(solution)/shard_map/ppermute | solution.py:22
  296.9 23.3 %collective-permute-start.8 = (bf16[640,8,1]{0,1,2:T(8,128)(2,1)S(1)}, bf16[640,8,1]{0,1,2:T(8,128)(2,1)S(1)}, u32[]{:S(2)}, u32[]{:S(2)}) collective-permute-start(bf16[640,8,1]{0,1,2:T(8,128)(2,1)S(1)} %copy.155), channel_id=1, source_target_pairs={{0,1},{2,3},{4,5},{6,7},{8,9},{10,11},{12,13},{14,15},{16,17},{18,... | collective-permute-start | bytes 30728 | tf_op jit(solution)/shard_map/ppermute | solution.py:21
  298.6 22.3 %collective-permute-start.9 = (bf16[640,8,1]{0,1,2:T(8,128)(2,1)S(1)}, bf16[640,8,1]{0,1,2:T(8,128)(2,1)S(1)}, u32[]{:S(2)}, u32[]{:S(2)}) collective-permute-start(bf16[640,8,1]{0,1,2:T(8,128)(2,1)S(1)} %copy.159), channel_id=1, source_target_pairs={{1,0},{3,2},{5,4},{7,6},{9,8},{11,10},{13,12},{15,14},{17,16},{19,... | collective-permute-start | bytes 30728 | tf_op jit(solution)/shard_map/ppermute | solution.py:22
  361.7 24.5 %collective-permute-start.13 = (bf16[4,2,80,6,128]{4,2,3,1,0:T(8,128)(2,1)S(1)}, bf16[4,2,80,6,128]{4,2,3,1,0:T(8,128)(2,1)S(1)}, u32[]{:S(2)}, u32[]{:S(2)}) collective-permute-start(bf16[4,2,80,6,128]{4,2,3,1,0:T(8,128)(2,1)S(1)} %constant_dynamic-slice_fusion), channel_id=1, source_target_pairs={{0,2},{2,0},{1,3},{3,1},{4,6},{6,4},{5,7},{7,5},{8,10},{10,8},{9,1... | collective-permute-start | bytes 2949128 | tf_op jit(solution)/shard_map/ppermute | solution.py:49
  (22 other events, 52.8 us)
Sparse Core Ops, SparseCore 0:
  9.0 75.1 all-gather.6
  85.8 70.9 all-gather.4
